TPU v7x, 128 devices: a whole 4x4x4 slice. The times are simulated.
128 devices in a mesh: row: 8 (over y, z_hi), col: 16 (over z_lo, x, core).
Axes of the slice: x: 4, y: 4, z: 4 (z_hi: 2, z_lo: 2; z = z_hi * 2 + z_lo), core: 2. Of those that a mesh axis runs over, the one named last changes fastest.
Arguments:
- upper_stored: bfloat16 [6144, 6144], P('row', 'col'), may hold values from -6 to 6
- block_cells: int32 [96, 3], replicated, may hold values from 0 to 15
Outputs:
- purified: bfloat16 [6144, 6144], P('row', 'col')
Inputs may be any that keep to these rules, and one draw needn't show every extreme that they name: `block_cells`: integer cell coordinates of each atom block on a periodic lattice of 16 cells a side.
All inputs are finite; a program needn't handle non-finite values.
Results may differ from a plain program's by a relative error of at most 0.0067.
Values may be sent and summed in bfloat16 or wider, within the bound.
No kernel may reach another device: no remote copies, remote signals or barrier semaphores. Data moves between devices by JAX's collectives and lax.ppermute only.
A program may use at most 64 MiB of HBM per device.

v0:
```python
import math
import jax
import jax.numpy as jnp
from jax import lax
from jax.sharding import PartitionSpec as P

BLK = 64
BOX = 16
NEAR = 40
FAR = 90


def cell_mask(block_cells, row_start, row_count, col_start, col_count, bound_sq):
    row_cells = lax.dynamic_slice_in_dim(block_cells, row_start, row_count, 0)
    col_cells = lax.dynamic_slice_in_dim(block_cells, col_start, col_count, 0)
    offset_abs = jnp.abs(row_cells[:, None, :] - col_cells[None, :, :])
    wrapped = jnp.minimum(offset_abs, BOX - offset_abs)
    return jnp.sum(wrapped * wrapped, axis=2) <= bound_sq


def block_keep(matrix_tile, keep_mask):
    row_count, col_count = matrix_tile.shape
    row_blocks, col_blocks = keep_mask.shape
    shaped = matrix_tile.reshape(
        row_blocks, row_count // row_blocks, col_blocks, col_count // col_blocks
    )
    kept = jnp.where(keep_mask[:, None, :, None], shaped, jnp.zeros_like(shaped))
    return kept.reshape(row_count, col_count)


def mirror_tile(upper_stored, rows, cols):
    tile_side, half_width = upper_stored.shape
    row_id = lax.axis_index("row")
    col_id = lax.axis_index("col")
    pieces = []
    for k in range(2):
        half = (col_id + k) % 2
        piece = lax.dynamic_slice_in_dim(upper_stored, half * half_width, half_width, 0)
        pairs = []
        for a in range(rows):
            for b in range(cols):
                h = (b + k) % 2
                pairs.append((a * cols + b, b // 2 * cols + 2 * a + h))
        pieces.append(lax.ppermute(piece, ("row", "col"), pairs))
    h_own = col_id % 2
    first = jnp.where(h_own == 0, pieces[0], pieces[1])
    second = jnp.where(h_own == 0, pieces[1], pieces[0])
    return jnp.concatenate([first, second], 1).T


def per_device(upper_stored, block_cells):
    rows = lax.axis_size("row")
    cols = lax.axis_size("col")
    row_id = lax.axis_index("row")
    col_id = lax.axis_index("col")
    tile_side, half_width = upper_stored.shape
    order_total = tile_side * rows
    tile_blocks = tile_side // BLK
    half_blocks = half_width // BLK
    mirrored = mirror_tile(upper_stored, rows, cols)
    global_rows = row_id * tile_side + lax.broadcasted_iota(jnp.int32, (tile_side, half_width), 0)
    global_cols = col_id * half_width + lax.broadcasted_iota(jnp.int32, (tile_side, half_width), 1)
    symmetric = jnp.where(global_rows <= global_cols, upper_stored, mirrored)
    near_own = cell_mask(
        block_cells, row_id * tile_blocks, tile_blocks, col_id * half_blocks, half_blocks, NEAR
    )
    far_own = cell_mask(
        block_cells, row_id * tile_blocks, tile_blocks, col_id * half_blocks, half_blocks, FAR
    )
    diagonal = jnp.where(global_rows == global_cols, 0.5, 0.0).astype(jnp.float32)
    value_scale = 2.0 / math.sqrt(order_total)
    density = block_keep(diagonal + value_scale * symmetric.astype(jnp.float32), near_own).astype(
        jnp.bfloat16
    )
    row_panel = lax.all_gather(density, "col", axis=1, tiled=True)
    col_panel = lax.all_gather(density, "row", axis=0, tiled=True)
    square = block_keep(jnp.dot(row_panel, col_panel, preferred_element_type=jnp.float32), far_own)
    square_low = square.astype(jnp.bfloat16)
    low_panel = lax.all_gather(square_low, "col", axis=1, tiled=True)
    cubic = jnp.dot(low_panel, col_panel, preferred_element_type=jnp.float32)
    return block_keep(3.0 * square - 2.0 * cubic, near_own).astype(jnp.bfloat16)


def solution(mesh):
    return jax.shard_map(
        per_device,
        mesh=mesh,
        in_specs=(P("row", "col"), P()),
        out_specs=P("row", "col"),
        check_vma=False,
    )
```

profile of v0, /device:TPU:1, one launch (start us, length us, event | category | flops | bytes accessed | tf_op | source)
XLA Modules:
  0.0 260.0 jit_solution(1769030043585015134)
XLA Ops:
  6.5 1.1 constant_dynamic-slice_fusion.1
  7.7 0.2 copy.16
  7.9 1.5 collective-permute-start.1
  9.3 0.2 copy.15
  9.6 0.7 collective-permute-start
  10.3 0.1 constant_dynamic-slice_fusion.2
  10.3 0.1 constant_dynamic-slice_fusion.3
  10.4 0.1 fusion.4
  10.5 0.1 copy.11
  10.6 0.3 broadcast_in_dim.35
  10.9 1.4 broadcast_in_dim.36
  12.4 0.1 broadcast_select_fusion.1
  12.4 1.3 select_convert_fusion
  13.8 0.0 all-gather.4.cloned.1.call-start
  13.9 0.7 all-gather.4.cloned.1.call-update
  14.6 0.0 all-gather.8.cloned.1.call-start
  14.6 0.1 copy.12
  14.7 0.3 broadcast_in_dim.37
  15.0 1.4 broadcast_in_dim.38
  16.4 102.2 %all-gather.6.cloned.1.call-done = bf16[6144,384]{1,0:T(8,128)(2,1)} async-done(((bf16[768,384]{1,0:T(8,128)(2,1)}), bf16[6144,384]{1,0:T(8,128)(2,1)}) %all-gather.6.cloned.1.call-update) | async-done | bytes 4718608 | tf_op jit(solution)/shard_map/all_gather | solution.py:76
  118.6 57.4 %all-gather.4.cloned.1.call-done = bf16[768,6144]{1,0:T(8,128)(2,1)} async-done(((bf16[768,384]{1,0:T(8,128)(2,1)}), bf16[768,6144]{1,0:T(8,128)(2,1)}) %all-gather.4.cloned.1.call-update) | async-done | bytes 9437200 | tf_op jit(solution)/shard_map/all_gather | solution.py:75
  176.0 9.7 %fusion.5 = (bf16[768,384]{1,0:T(8,128)(2,1)}, f32[768,384]{1,0:T(8,128)S(1)}) fusion(pred[768,384]{1,0:T(32,128)(4,1)S(1)} %broadcast_in_dim.38, bf16[768,6144]{1,0:T(8,128)(2,1)} %all-gather.4.cloned.1.call-done, bf16[6144,384]{1,0:T(8,128)(2,1)} %all-gather.6.cloned.1.call-done), kind=kOutput, calls=%fused_computation.21 | convolution fusion | flops 3624468480 | bytes 16220160 | tf_op jit(solution)/shard_map/dot_general | solution.py:77
  185.7 58.0 %all-gather.8.cloned.1.call-done = bf16[768,6144]{1,0:T(8,128)(2,1)} async-done(((bf16[768,384]{1,0:T(8,128)(2,1)}), bf16[768,6144]{1,0:T(8,128)(2,1)}) %all-gather.8.cloned.1.call-update) | async-done | bytes 9437200 | tf_op jit(solution)/shard_map/all_gather | solution.py:79
  243.7 9.7 %fusion.2 = bf16[768,384]{1,0:T(8,128)(2,1)} fusion(pred[768,384]{1,0:T(32,128)(4,1)S(1)} %broadcast_in_dim.36, bf16[768,6144]{1,0:T(8,128)(2,1)} %all-gather.8.cloned.1.call-done, bf16[6144,384]{1,0:T(8,128)(2,1)} %all-gather.6.cloned.1.call-done, f32[768,384]{1,0:T(8,128)S(1)} %get-tuple-element.12), kind=kOutput, calls=%fused_computation.4 | convolution fusion | flops 3625353216 | bytes 16220160 | tf_op jit(solution)/shard_map/dot_general | solution.py:80
  (12 shorter events, 0.1 us)
Async XLA Ops:
  6.5 3.7 %copy-start = (s32[96,3]{0,1:T(4,128)S(1)}, s32[96,3]{0,1:T(4,128)}, u32[]{:S(2)}) copy-start(s32[96,3]{0,1:T(4,128)} %param.3) | copy-start | bytes 3460
  6.5 112.0 %all-gather.6.cloned.1.call-start = ((), (), s32[]{:S(2)}) async-start(), calls=%async_computation.1 | async-start | bytes 5308416 | tf_op jit(solution)/shard_map/all_gather | solution.py:76
  7.9 4.5 %collective-permute-start.1 = (bf16[384,384]{0,1:T(8,128)(2,1)S(1)}, bf16[384,384]{0,1:T(8,128)(2,1)S(1)}, u32[]{:S(2)}, u32[]{:S(2)}) collective-permute-start(bf16[384,384]{0,1:T(8,128)(2,1)S(1)} %copy.16), channel_id=1, source_target_pairs={{0,1},{1,0},{2,17},{3,16},{4,33},{5,32},{6,49},{7,48},{8,65},{9,64... | collective-permute-start | bytes 884744 | tf_op jit(solution)/shard_map/ppermute | solution.py:44
  9.6 2.8 %collective-permute-start = (bf16[384,384]{0,1:T(8,128)(2,1)S(1)}, bf16[384,384]{0,1:T(8,128)(2,1)S(1)}, u32[]{:S(2)}, u32[]{:S(2)}) collective-permute-start(bf16[384,384]{0,1:T(8,128)(2,1)S(1)} %copy.15), channel_id=1, source_target_pairs={{0,0},{1,1},{2,16},{3,17},{4,32},{5,33},{6,48},{7,49},{8,64},{9,65... | collective-permute-start | bytes 884744 | tf_op jit(solution)/shard_map/ppermute | solution.py:44
  10.9 1.5 copy-start.1
  13.8 162.2 %all-gather.4.cloned.1.call-start = ((), (), s32[]{:S(2)}) async-start(), calls=%async_computation | async-start | bytes 10027008 | tf_op jit(solution)/shard_map/all_gather | solution.py:75
  14.6 229.1 %all-gather.8.cloned.1.call-start = ((), (), s32[]{:S(2)}) async-start(), calls=%async_computation.2 | async-start | bytes 10027008 | tf_op jit(solution)/shard_map/all_gather | solution.py:79
Sparse Core Ops, SparseCore 0:
  13.9 104.6 all-gather.5
  120.2 55.7 all-gather.3
  185.9 57.7 all-gather.7
where the time goes:
time: 260 us
  waiting for transfers between devices  218 us (84%)
  matrix products  19.4 us (7%)
  between operations  13.2 us (5%)
  local copies, waits for them, and re-layouts  5.25 us (2%)
    all_gather x1, waiting for transfers between devices, per_device(): col_panel = lax.all_gather(density, 'row', axis=0, tiled=True)  102 us
    all_gather x1, waiting for transfers between devices, per_device(): low_panel = lax.all_gather(square_low, 'col', axis=1, tiled=True)  58 us
    all_gather x1, waiting for transfers between devices, per_device(): row_panel = lax.all_gather(density, 'col', axis=1, tiled=True)  57.4 us
    dot_general x1, matrix products, per_device(): cubic = jnp.dot(low_panel, col_panel, preferred_element_type=jnp.float32)  9.75 us
    dot_general x1, matrix products, per_device(): jnp.dot(row_panel, col_panel, preferred_element_type=jnp.float32)  9.69 us
  transfers between devices with their start and end apart: 5, of which 3 were waited for; matrix products, arithmetic and copies ran while one was open for 2% of the time, Pallas kernels for 0%

commit v1 on v0

--- a/solution.py
+++ b/solution.py
@@ -76,7 +76,9 @@
     col_panel = lax.all_gather(density, "row", axis=0, tiled=True)
     square = block_keep(jnp.dot(row_panel, col_panel, preferred_element_type=jnp.float32), far_own)
     square_low = square.astype(jnp.bfloat16)
-    low_panel = lax.all_gather(square_low, "col", axis=1, tiled=True)
+    low_panel = jnp.concatenate(
+        lax.all_to_all(jnp.stack([square_low] * lax.axis_size("col")), "col", 0, 0), axis=1
+    )
     cubic = jnp.dot(low_panel, col_panel, preferred_element_type=jnp.float32)
     return block_keep(3.0 * square - 2.0 * cubic, near_own).astype(jnp.bfloat16)
 

time: 260 us -> 311 us (1.20)
  blocking collectives: 0 us -> 110 us
  waiting for transfers between devices: 218 us -> 160 us
    all_to_all x0 -> x1, blocking collectives: none -> 110 us  [per_device(): lax.all_to_all(jnp.stack([square_low] * lax.axis_size('col')), 'col', 0, 0)]
    all_gather x1 -> x0, waiting for transfers between devices: 58 us -> none  [per_device(): low_panel = lax.all_gather(square_low, 'col', axis=1, tiled=True)]
  transfers between devices with their start and end apart: 5 -> 4, of which waited for: 3 -> 2; matrix products, arithmetic and copies ran while one was open for 2% -> 1% of each run, Pallas kernels for 0% -> 0%
where the time goes in v1:
time: 311 us
  waiting for transfers between devices  160 us (51%)
  blocking collectives  110 us (35%)
  matrix products  17.3 us (6%)
  between operations  13.5 us (4%)
  local copies, waits for them, and re-layouts  6.41 us (2%)
    all_to_all x1, blocking collectives, per_device(): lax.all_to_all(jnp.stack([square_low] * lax.axis_size('col')), 'col', 0, 0)  110 us
    all_gather x1, waiting for transfers between devices, per_device(): col_panel = lax.all_gather(density, 'row', axis=0, tiled=True)  102 us
    all_gather x1, waiting for transfers between devices, per_device(): row_panel = lax.all_gather(density, 'col', axis=1, tiled=True)  57.4 us
    dot_general x1, matrix products, per_device(): jnp.dot(row_panel, col_panel, preferred_element_type=jnp.float32)  8.99 us
    dot_general x1, matrix products, per_device(): cubic = jnp.dot(low_panel, col_panel, preferred_element_type=jnp.float32)  8.26 us
  transfers between devices with their start and end apart: 4, of which 2 were waited for; matrix products, arithmetic and copies ran while one was open for 1% of the time, Pallas kernels for 0%

profile of v1, /device:TPU:1, one launch (start us, length us, event | category | flops | bytes accessed | tf_op | source)
XLA Modules:
  0.0 311.2 jit_solution(3293001950741108667)
XLA Ops:
  6.5 1.1 constant_dynamic-slice_fusion.1
  7.7 0.2 copy.18
  7.9 1.5 collective-permute-start.1
  9.3 0.2 copy.17
  9.6 0.7 collective-permute-start
  10.3 0.1 constant_dynamic-slice_fusion.2
  10.3 0.1 constant_dynamic-slice_fusion.3
  10.4 0.1 fusion.4
  10.5 0.1 copy.12
  10.6 0.3 broadcast_in_dim.35
  10.9 1.4 broadcast_in_dim.36
  12.4 0.1 broadcast_select_fusion.1
  12.4 1.3 select_convert_fusion
  13.9 0.7 all-gather.3.cloned.1.call-update
  14.6 0.1 copy.13
  14.7 0.3 broadcast_in_dim.37
  14.9 1.4 broadcast_in_dim.38
  16.3 102.2 %all-gather.5.cloned.1.call-done = bf16[6144,384]{1,0:T(8,128)(2,1)} async-done(((bf16[768,384]{1,0:T(8,128)(2,1)}), bf16[6144,384]{1,0:T(8,128)(2,1)}) %all-gather.5.cloned.1.call-update) | async-done | bytes 4718608 | tf_op jit(solution)/shard_map/all_gather | solution.py:76
  118.6 57.4 %all-gather.3.cloned.1.call-done = bf16[768,6144]{1,0:T(8,128)(2,1)} async-done(((bf16[768,384]{1,0:T(8,128)(2,1)}), bf16[768,6144]{1,0:T(8,128)(2,1)}) %all-gather.3.cloned.1.call-update) | async-done | bytes 9437200 | tf_op jit(solution)/shard_map/all_gather | solution.py:75
  176.0 9.0 %fusion.5 = (bf16[768,384]{1,0:T(8,128)(2,1)S(1)}, f32[768,384]{1,0:T(8,128)S(1)}) fusion(pred[768,384]{1,0:T(32,128)(4,1)S(1)} %broadcast_in_dim.38, bf16[768,6144]{1,0:T(8,128)(2,1)} %all-gather.3.cloned.1.call-done, bf16[6144,384]{1,0:T(8,128)(2,1)} %all-gather.5.cloned.1.call-done), kind=kOutput, calls=%fused_computation.21 | convolution fusion | flops 3624468480 | bytes 16220160 | tf_op jit(solution)/shard_map/dot_general | solution.py:77
  185.0 0.3 copy.16
  185.3 0.9 stack.2
  186.2 109.9 %all_to_all.5 = bf16[16,768,384]{1,2,0:T(8,128)(2,1)S(1)} all-to-all(bf16[16,768,384]{1,2,0:T(8,128)(2,1)S(1)} %stack.2), channel_id=1, replica_groups=mesh['row'=8,'col'=16] {'col'}, dimensions={0} | all-to-all | bytes 18874368 | tf_op jit(solution)/shard_map/all_to_all | solution.py:80
  296.1 8.3 %fusion.2 = bf16[768,384]{1,0:T(8,128)(2,1)} fusion(pred[768,384]{1,0:T(32,128)(4,1)S(1)} %broadcast_in_dim.36, bf16[768,6144]{0,1:T(8,128)(2,1)S(1)} %bitcast.11, bf16[6144,384]{1,0:T(8,128)(2,1)} %all-gather.5.cloned.1.call-done, f32[768,384]{1,0:T(8,128)S(1)} %get-tuple-element.12), kind=kOutput, calls=%fused_computation.4 | convolution fusion | flops 3625353216 | bytes 16220160 | tf_op jit(solution)/shard_map/dot_general | solution.py:82
  (12 shorter events, 0.1 us)
Async XLA Ops:
  6.5 3.7 %copy-start = (s32[96,3]{0,1:T(4,128)S(1)}, s32[96,3]{0,1:T(4,128)}, u32[]{:S(2)}) copy-start(s32[96,3]{0,1:T(4,128)} %param.3) | copy-start | bytes 3460
  6.5 112.0 %all-gather.5.cloned.1.call-start = ((), (), s32[]{:S(2)}) async-start(), calls=%async_computation.2 | async-start | bytes 5308416 | tf_op jit(solution)/shard_map/all_gather | solution.py:76
  7.9 4.5 %collective-permute-start.1 = (bf16[384,384]{0,1:T(8,128)(2,1)S(1)}, bf16[384,384]{0,1:T(8,128)(2,1)S(1)}, u32[]{:S(2)}, u32[]{:S(2)}) collective-permute-start(bf16[384,384]{0,1:T(8,128)(2,1)S(1)} %copy.18), channel_id=1, source_target_pairs={{0,1},{1,0},{2,17},{3,16},{4,33},{5,32},{6,49},{7,48},{8,65},{9,64... | collective-permute-start | bytes 884744 | tf_op jit(solution)/shard_map/ppermute | solution.py:44
  9.6 2.8 collective-permute-start
  10.9 1.5 copy-start.1
  13.8 162.2 %all-gather.3.cloned.1.call-start = ((), (), s32[]{:S(2)}) async-start(), calls=%async_computation.1 | async-start | bytes 10027008 | tf_op jit(solution)/shard_map/all_gather | solution.py:75
Sparse Core Ops, SparseCore 0:
  13.9 104.6 all-gather.4
  120.2 55.7 all-gather.2
